TPU v7x, 32 devices: a whole 2x2x4 slice. The times are simulated.
32 devices in a mesh: src: 2 (over core), rows: 16 (over z, y, x).
Axes of the slice: x: 2, y: 2, z: 4, core: 2. Of those that a mesh axis runs over, the one named last changes fastest.
Arguments:
- slip_units: int32 [512, 2000], P(None, 'src'), may hold values from 0 to 15
- slip_scales: float32 [512, 16], P(None, 'src'), may hold values from 0.02 to 0.2
- green: bfloat16 [2000, 491520], P('src', 'rows'), may hold values from -0.08944272 to 0.08944272
- coast_gauges: int32 [2048, 8], replicated, may hold values from 0 to 2047
- coast_amps: float32 [2048, 8], replicated, may hold values from 0.05 to 0.3
- coast_counts: int32 [2048], replicated, may hold values from 1 to 8
Outputs:
- onshore: float32 [512, 2048], P('src', 'rows')
Inputs may be any that keep to these rules, and one draw needn't show every extreme that they name: coast_gauges names gauges.
All inputs are finite; a program needn't handle non-finite values.
Results may differ from a plain program's by a relative error of at most 0.0039.
Values may be sent and summed in bfloat16 or wider, within the bound.
No kernel may reach another device: no remote copies, remote signals or barrier semaphores. Data moves between devices by JAX's collectives and lax.ppermute only.
A program may use at most 192 MiB of HBM per device.

v0:
```python
import jax
import jax.numpy as jnp
from jax import lax
from jax.sharding import PartitionSpec as P

NT = 240
UBLK = 125


def body(slip_units, slip_scales, green, coast_gauges, coast_amps, coast_counts):
    scenarios = slip_units.shape[0]
    sources_here = slip_units.shape[1]
    block_count = slip_scales.shape[1]
    slip_weights = (
        (
            slip_units.astype(jnp.float32).reshape(scenarios, block_count, UBLK)
            * slip_scales[:, :, None]
        )
        .reshape(scenarios, sources_here)
        .astype(jnp.bfloat16)
    )
    columns = green.shape[1]
    gauge_count = columns // NT
    groups = lax.axis_size("src")
    portion = scenarios // groups
    waveforms = lax.psum_scatter(
        jnp.dot(slip_weights, green, preferred_element_type=jnp.float32).astype(jnp.bfloat16),
        "src",
        scatter_dimension=0,
        tiled=True,
    ).astype(jnp.float32)
    peak_values = jnp.max(jnp.abs(waveforms.reshape(portion, gauge_count, NT)), axis=2)
    tile_total = coast_gauges.shape[0]
    slot_count = coast_gauges.shape[1]
    owners = lax.axis_size("rows")
    tiles_here = tile_total // owners
    active_slot = jnp.arange(slot_count, dtype=jnp.int32)[None, :] < coast_counts[:, None]
    weights = jnp.where(active_slot, coast_amps, jnp.zeros_like(coast_amps))
    gathered = lax.all_gather(peak_values, "rows", axis=1, tiled=True)
    first_tile = lax.axis_index("rows") * tiles_here
    mine_gauges = lax.dynamic_slice_in_dim(coast_gauges, first_tile, tiles_here, 0)
    mine_weights = lax.dynamic_slice_in_dim(weights, first_tile, tiles_here, 0)
    matches = (
        mine_gauges[:, :, None] == jnp.arange(gauge_count * owners, dtype=jnp.int32)[None, None, :]
    )
    tile_table = jnp.sum(jnp.where(matches, mine_weights[:, :, None], 0.0), axis=1)
    onshore = lax.dot_general(
        gathered,
        tile_table,
        (((1,), (1,)), ((), ())),
        precision=lax.Precision.HIGHEST,
        preferred_element_type=jnp.float32,
    )
    return onshore


def solution(mesh):
    in_specs = (P(None, "src"), P(None, "src"), P("src", "rows"), P(), P(), P())
    out_specs = P("src", "rows")
    return jax.shard_map(body, mesh=mesh, in_specs=in_specs, out_specs=out_specs, check_vma=False)
```

profile of v0, /device:TPU:0, one launch (start us, length us, event | category | flops | bytes accessed | tf_op | source)
XLA Modules:
  0.0 232.7 jit_solution(9461021766356233926)
XLA Ops:
  6.5 0.0 copy-start
  6.5 0.0 reduce-scatter.2.cloned.1.call-start
  6.5 1.0 mul.14
  7.5 1.6 mul.15
  9.1 43.3 %convolution_convert_fusion = bf16[512,30720]{1,0:T(8,128)(2,1)} fusion(bf16[1000,30720]{1,0:T(8,128)(2,1)} %param.8, f32[512,1000]{0,1:T(8,128)} %mul.15, s32[512,1000]{0,1:T(8,128)} %param.6), kind=kOutput, calls=%fused_computation | convolution fusion | flops 31474544640 | bytes 96993280 | tf_op jit(solution)/shard_map/dot_general | solution.py:27
  52.4 0.0 reduce-scatter.2.cloned.1.call-update
  52.4 0.2 all-gather.2.cloned.1.call-start
  52.6 45.3 %reduce-scatter.2.cloned.1.call-done = bf16[256,30720]{1,0:T(8,128)(2,1)} async-done(((bf16[512,30720]{1,0:T(8,128)(2,1)}), bf16[256,30720]{1,0:T(8,128)(2,1)}) %reduce-scatter.2.cloned.1.call-update) | async-done | bytes 15728656 | tf_op jit(solution)/shard_map/reduce_scatter | solution.py:26
  97.9 17.5 %convert_abs_fusion = f32[256,30720]{1,0:T(8,128)} fusion(bf16[256,30720]{1,0:T(8,128)(2,1)} %reduce-scatter.2.cloned.1.call-done), kind=kLoop, calls=%fused_computation.1 | loop fusion | flops 15728640 | bytes 47185920 | tf_op jit(solution)/shard_map/abs | solution.py:32
  115.5 30.7 %copy.15 = f32[256,30720]{0,1:T(8,128)} copy(f32[256,30720]{1,0:T(8,128)} %convert_abs_fusion) | data formatting | bytes 62914560 | tf_op jit(solution)/shard_map/abs | solution.py:32
  146.1 12.0 %reduce_max.9 = f32[256,128]{0,1:T(8,128)} reduce(f32[256,128,240]{0,2,1:T(8,128)} %bitcast.7, f32[]{:T(128)} %constant.6.clone.1), dimensions={2}, to_apply=%region_1.0 | reduce | flops 7831552 | bytes 31588356 | tf_op jit(solution)/shard_map/reduce_max | solution.py:32
  158.1 0.0 all-gather.2.cloned.1.call-update
  158.1 0.8 dynamic-slice
  158.9 0.7 dynamic-slice_select_fusion
  159.6 0.1 copy.17
  159.7 0.0 copy-done
  159.7 0.1 copy.16
  159.8 2.7 %select_reduce_fusion = f32[128,2048]{1,0:T(8,128)S(1)} fusion(f32[128,8]{1,0:T(8,128)S(1)} %copy.17, s32[128,8]{1,0:T(8,128)S(1)} %copy.16), kind=kLoop, calls=%fused_computation.2 | loop fusion | flops 6029312 | bytes 1056768 | tf_op jit(solution)/shard_map/reduce_sum | solution.py:46
  162.6 57.6 %all-gather.2.cloned.1.call-done = f32[256,2048]{0,1:T(8,128)} async-done(((f32[256,128]{0,1:T(8,128)}), f32[256,2048]{0,1:T(8,128)}) %all-gather.2.cloned.1.call-update) | async-done | bytes 2097168 | tf_op jit(solution)/shard_map/all_gather | solution.py:39
  220.2 5.7 %fusion = f32[256,128]{1,0:T(8,128)} fusion(f32[256,2048]{0,1:T(8,128)} %all-gather.2.cloned.1.call-done, f32[128,2048]{1,0:T(8,128)S(1)} %select_reduce_fusion), kind=kOutput, calls=%fused_computation.8 | convolution fusion | flops 805306368 | bytes 3276800 | tf_op jit(solution)/shard_map/dot_general | solution.py:47
  (1 shorter events, 0.0 us)
Async XLA Ops:
  6.5 153.2 %copy-start = (s32[2048,8]{0,1:T(8,128)S(1)}, s32[2048,8]{0,1:T(8,128)}, u32[]{:S(2)}) copy-start(s32[2048,8]{0,1:T(8,128)} %param.9) | copy-start | bytes 196612
  6.5 91.4 %reduce-scatter.2.cloned.1.call-start = ((), (), s32[]{:S(2)}) async-start(), calls=%async_computation.1 | async-start | bytes 47185920 | tf_op jit(solution)/shard_map/reduce_scatter | solution.py:26
  52.4 167.7 %all-gather.2.cloned.1.call-start = ((), (), s32[]{:S(2)}) async-start(), calls=%async_computation.2 | async-start | bytes 2228224 | tf_op jit(solution)/shard_map/all_gather | solution.py:39
Sparse Core Ops, SparseCore 0:
  52.5 45.3 reduce-scatter.1
  158.3 61.8 all-gather.1
where the time goes:
time: 233 us
  waiting for transfers between devices  103 us (44%)
  matrix products  48.9 us (21%)
  local copies, waits for them, and re-layouts  34.2 us (15%)
  other arithmetic  32.9 us (14%)
  between operations  13.4 us (6%)
    all_gather x1, waiting for transfers between devices, body(): gathered = lax.all_gather(peak_values, 'rows', axis=1, tiled=True)  57.6 us
    reduce_scatter x1, waiting for transfers between devices, body(): lax.psum_scatter(jnp.dot(slip_weights, green, preferred_element_type=jnp....  45.3 us
    dot_general x1, matrix products, body(): jnp.dot(slip_weights, green, preferred_element_type=jnp.float32)  43.3 us
    abs x1, local copies, waits for them, and re-layouts, body(): jnp.abs(waveforms.reshape(portion, gauge_count, NT))  30.7 us
    abs x1, other arithmetic, body(): jnp.abs(waveforms.reshape(portion, gauge_count, NT))  17.5 us
    reduce_max x1, other arithmetic, body(): jnp.max(jnp.abs(waveforms.reshape(portion, gauge_count, NT)), axis=2)  12 us
    dot_general x1, matrix products, body(): lax.dot_general(gathered, tile_table, (((1,), (1,)), ((), ())), precision...  5.67 us
  transfers between devices with their start and end apart: 2, of which 2 were waited for; matrix products, arithmetic and copies ran while one was open for 2% of the time, Pallas kernels for 0%

commit v1 on v0

--- a/solution.py
+++ b/solution.py
@@ -5,6 +5,18 @@
 
 NT = 240
 UBLK = 125
+
+
+def gather_by_bits(array, axis, dim):
+    ways, here = (lax.axis_size(axis), lax.axis_index(axis))
+    grown, reach = (array, 1)
+    while reach < ways:
+        theirs = lax.ppermute(grown, axis, [(d, d ^ reach) for d in range(ways)])
+        mine_first = jnp.concatenate([grown, theirs], axis=dim)
+        theirs_first = jnp.concatenate([theirs, grown], axis=dim)
+        grown = jnp.where(here & reach == 0, mine_first, theirs_first)
+        reach = 2 * reach
+    return grown
 
 
 def body(slip_units, slip_scales, green, coast_gauges, coast_amps, coast_counts):
@@ -36,7 +48,7 @@
     tiles_here = tile_total // owners
     active_slot = jnp.arange(slot_count, dtype=jnp.int32)[None, :] < coast_counts[:, None]
     weights = jnp.where(active_slot, coast_amps, jnp.zeros_like(coast_amps))
-    gathered = lax.all_gather(peak_values, "rows", axis=1, tiled=True)
+    gathered = gather_by_bits(peak_values, "rows", 1)
     first_tile = lax.axis_index("rows") * tiles_here
     mine_gauges = lax.dynamic_slice_in_dim(coast_gauges, first_tile, tiles_here, 0)
     mine_weights = lax.dynamic_slice_in_dim(weights, first_tile, tiles_here, 0)

time: 233 us -> 242 us (1.039)
  starting transfers between devices: 0.22 us -> 8.02 us
    ppermute x0 -> x4, waiting for transfers between devices: none -> 59.6 us  [gather_by_bits(): theirs = lax.ppermute(grown, axis, [(d, d ^ reach) for d in range(ways)])]
    all_gather x1 -> x0, waiting for transfers between devices: 57.6 us -> none  [body(): gathered = lax.all_gather(peak_values, 'rows', axis=1, tiled=True)]
    ppermute x0 -> x4, starting transfers between devices: none -> 8.02 us  [gather_by_bits(): theirs = lax.ppermute(grown, axis, [(d, d ^ reach) for d in range(ways)])]
  transfers between devices with their start and end apart: 2 -> 5, of which waited for: 2 -> 5; matrix products, arithmetic and copies ran while one was open for 2% -> 2% of each run, Pallas kernels for 0% -> 0%
where the time goes in v1:
time: 242 us; the launch traced here: 241 us
  waiting for transfers between devices  105 us (43%)
  matrix products  47.4 us (20%)
  local copies, waits for them, and re-layouts  34.2 us (14%)
  other arithmetic  32.6 us (13%)
  between operations  13.5 us (6%)
  starting transfers between devices  8.02 us (3%)
    ppermute x4, waiting for transfers between devices, gather_by_bits(): theirs = lax.ppermute(grown, axis, [(d, d ^ reach) for d in range(ways)])  59.6 us
    reduce_scatter x1, waiting for transfers between devices, body(): lax.psum_scatter(jnp.dot(slip_weights, green, preferred_element_type=jnp....  45.5 us
    dot_general x1, matrix products, body(): jnp.dot(slip_weights, green, preferred_element_type=jnp.float32)  43.3 us
    abs x1, local copies, waits for them, and re-layouts, body(): jnp.abs(waveforms.reshape(portion, gauge_count, NT))  30.7 us
    abs x1, other arithmetic, body(): jnp.abs(waveforms.reshape(portion, gauge_count, NT))  17.5 us
    reduce_max x1, other arithmetic, body(): jnp.max(jnp.abs(waveforms.reshape(portion, gauge_count, NT)), axis=2)  11.3 us
    ppermute x4, starting transfers between devices, gather_by_bits(): theirs = lax.ppermute(grown, axis, [(d, d ^ reach) for d in range(ways)])  8.02 us
  transfers between devices with their start and end apart: 5, of which 5 were waited for; matrix products, arithmetic and copies ran while one was open for 2% of the time, Pallas kernels for 0%

profile of v1, /device:TPU:0, one launch (start us, length us, event | category | flops | bytes accessed | tf_op | source)
XLA Modules:
  0.0 240.9 jit_solution(12938783877304440868)
XLA Ops:
  6.5 0.0 copy-start
  6.5 0.0 reduce-scatter.2.cloned.1.call-start
  6.5 1.0 mul.14
  7.5 1.6 mul.15
  9.1 43.3 %convolution_convert_fusion = bf16[512,30720]{1,0:T(8,128)(2,1)} fusion(bf16[1000,30720]{1,0:T(8,128)(2,1)} %param.8, f32[512,1000]{0,1:T(8,128)} %mul.15, s32[512,1000]{0,1:T(8,128)} %param.6), kind=kOutput, calls=%fused_computation | convolution fusion | flops 31474544640 | bytes 96993280 | tf_op jit(solution)/shard_map/dot_general | solution.py:39
  52.4 0.0 reduce-scatter.2.cloned.1.call-update
  52.4 45.5 %reduce-scatter.2.cloned.1.call-done = bf16[256,30720]{1,0:T(8,128)(2,1)} async-done(((bf16[512,30720]{1,0:T(8,128)(2,1)}), bf16[256,30720]{1,0:T(8,128)(2,1)}) %reduce-scatter.2.cloned.1.call-update) | async-done | bytes 15728656 | tf_op jit(solution)/shard_map/reduce_scatter | solution.py:38
  97.9 17.5 %convert_abs_fusion = f32[256,30720]{1,0:T(8,128)} fusion(bf16[256,30720]{1,0:T(8,128)(2,1)} %reduce-scatter.2.cloned.1.call-done), kind=kLoop, calls=%fused_computation.1 | loop fusion | flops 15728640 | bytes 47185920 | tf_op jit(solution)/shard_map/abs | solution.py:44
  115.5 30.7 %copy.15 = f32[256,30720]{0,1:T(8,128)} copy(f32[256,30720]{1,0:T(8,128)} %convert_abs_fusion) | data formatting | bytes 62914560 | tf_op jit(solution)/shard_map/abs | solution.py:44
  146.1 11.3 %reduce_max.9 = f32[256,128]{0,1:T(8,128)S(1)} reduce(f32[256,128,240]{0,2,1:T(8,128)} %bitcast.6, f32[]{:T(128)} %constant.5.clone.1), dimensions={2}, to_apply=%region_1.0 | reduce | flops 7831552 | bytes 31588356 | tf_op jit(solution)/shard_map/reduce_max | solution.py:44
  157.5 1.8 collective-permute-start
  159.2 4.0 %collective-permute-done = f32[256,128]{0,1:T(8,128)S(1)} collective-permute-done((f32[256,128]{0,1:T(8,128)S(1)}, f32[256,128]{0,1:T(8,128)S(1)}, u32[]{:S(2)}, u32[]{:S(2)}) %collective-permute-start) | collective-permute-done | bytes 131104 | tf_op jit(solution)/shard_map/ppermute | solution.py:14
  163.3 1.8 collective-permute-start.1
  165.1 6.0 %collective-permute-done.1 = f32[256,256]{0,1:T(8,128)S(1)} collective-permute-done((f32[256,256]{0,1:T(8,128)S(1)}, f32[256,256]{0,1:T(8,128)S(1)}, u32[]{:S(2)}, u32[]{:S(2)}) %collective-permute-start.1) | collective-permute-done | bytes 262176 | tf_op jit(solution)/shard_map/ppermute | solution.py:14
  171.1 1.8 collective-permute-start.2
  172.9 10.7 %collective-permute-done.2 = f32[256,512]{0,1:T(8,128)S(1)} collective-permute-done((f32[256,512]{0,1:T(8,128)S(1)}, f32[256,512]{0,1:T(8,128)S(1)}, u32[]{:S(2)}, u32[]{:S(2)}) %collective-permute-start.2) | collective-permute-done | bytes 524320 | tf_op jit(solution)/shard_map/ppermute | solution.py:14
  183.6 0.1 maximum_select_fusion.2
  183.7 2.7 %collective-permute-start.3 = (f32[256,1024]{0,1:T(8,128)S(1)}, f32[256,1024]{0,1:T(8,128)S(1)}, u32[]{:S(2)}, u32[]{:S(2)}) collective-permute-start(f32[256,1024]{0,1:T(8,128)S(1)} %maximum_select_fusion.2), channel_id=1, source_target_pairs={{0,8},{1,9},{2,10},{3,11},{4,12},{5,13},{6,14},{7,15},{8,0},{9,1},... | collective-permute-start | bytes 3145736 | tf_op jit(solution)/shard_map/ppermute | solution.py:14
  186.4 0.8 dynamic-slice
  187.2 0.7 dynamic-slice_select_fusion
  187.9 0.1 copy.17
  188.0 0.0 copy-done
  188.0 0.1 copy.16
  188.1 2.9 %select_reduce_fusion = f32[128,2048]{1,0:T(8,128)S(1)} fusion(f32[128,8]{1,0:T(8,128)S(1)} %copy.17, s32[128,8]{1,0:T(8,128)S(1)} %copy.16), kind=kLoop, calls=%fused_computation.2 | loop fusion | flops 6029312 | bytes 1056768 | tf_op jit(solution)/shard_map/reduce_sum | solution.py:58
  191.0 38.9 %collective-permute-done.3 = f32[256,1024]{0,1:T(8,128)S(1)} collective-permute-done((f32[256,1024]{0,1:T(8,128)S(1)}, f32[256,1024]{0,1:T(8,128)S(1)}, u32[]{:S(2)}, u32[]{:S(2)}) %collective-permute-start.3) | collective-permute-done | bytes 1048608 | tf_op jit(solution)/shard_map/ppermute | solution.py:14
  229.9 4.1 %fusion = f32[256,128]{1,0:T(8,128)} fusion(f32[128,2048]{1,0:T(8,128)S(1)} %select_reduce_fusion, f32[256,1024]{0,1:T(8,128)S(1)} %collective-permute-done.3, f32[256,1024]{0,1:T(8,128)S(1)} %maximum_select_fusion.2, pred[]{:T(512)S(6)} %eq.25), kind=kOutput, calls=%fused_computation.5 | convolution fusion | flops 806879232 | bytes 3276801 | tf_op jit(solution)/shard_map/dot_general | solution.py:59
  (3 shorter events, 0.1 us)
Async XLA Ops:
  6.5 181.4 %copy-start = (s32[2048,8]{0,1:T(8,128)S(1)}, s32[2048,8]{0,1:T(8,128)}, u32[]{:S(2)}) copy-start(s32[2048,8]{0,1:T(8,128)} %param.9) | copy-start | bytes 196612
  6.5 91.4 %reduce-scatter.2.cloned.1.call-start = ((), (), s32[]{:S(2)}) async-start(), calls=%async_computation.1 | async-start | bytes 47185920 | tf_op jit(solution)/shard_map/reduce_scatter | solution.py:38
  157.5 5.8 %collective-permute-start = (f32[256,128]{0,1:T(8,128)S(1)}, f32[256,128]{0,1:T(8,128)S(1)}, u32[]{:S(2)}, u32[]{:S(2)}) collective-permute-start(f32[256,128]{0,1:T(8,128)S(1)} %reduce_max.9), channel_id=1, source_target_pairs={{0,1},{1,0},{2,3},{3,2},{4,5},{5,4},{6,7},{7,6},{8,9},{9,8},{10,11... | collective-permute-start | bytes 393224 | tf_op jit(solution)/shard_map/ppermute | solution.py:14
  163.3 7.8 %collective-permute-start.1 = (f32[256,256]{0,1:T(8,128)S(1)}, f32[256,256]{0,1:T(8,128)S(1)}, u32[]{:S(2)}, u32[]{:S(2)}) collective-permute-start(f32[256,256]{0,1:T(8,128)S(1)} %maximum_select_fusion.4), channel_id=1, source_target_pairs={{0,2},{1,3},{2,0},{3,1},{4,6},{5,7},{6,4},{7,5},{8,10},{9,11},{10,... | collective-permute-start | bytes 786440 | tf_op jit(solution)/shard_map/ppermute | solution.py:14
  171.1 12.5 %collective-permute-start.2 = (f32[256,512]{0,1:T(8,128)S(1)}, f32[256,512]{0,1:T(8,128)S(1)}, u32[]{:S(2)}, u32[]{:S(2)}) collective-permute-start(f32[256,512]{0,1:T(8,128)S(1)} %maximum_select_fusion.3), channel_id=1, source_target_pairs={{0,4},{1,5},{2,6},{3,7},{4,0},{5,1},{6,2},{7,3},{8,12},{9,13},{10,... | collective-permute-start | bytes 1572872 | tf_op jit(solution)/shard_map/ppermute | solution.py:14
  183.7 46.2 %collective-permute-start.3 = (f32[256,1024]{0,1:T(8,128)S(1)}, f32[256,1024]{0,1:T(8,128)S(1)}, u32[]{:S(2)}, u32[]{:S(2)}) collective-permute-start(f32[256,1024]{0,1:T(8,128)S(1)} %maximum_select_fusion.2), channel_id=1, source_target_pairs={{0,8},{1,9},{2,10},{3,11},{4,12},{5,13},{6,14},{7,15},{8,0},{9,1},... | collective-permute-start | bytes 3145736 | tf_op jit(solution)/shard_map/ppermute | solution.py:14
Sparse Core Ops, SparseCore 0:
  52.5 45.3 reduce-scatter.1
